TPU v7x, 256 devices: a whole 4x4x8 slice. The times are simulated.
256 devices in a mesh: dp: 16 (over y, x), section: 2 (over core), tensor: 8 (over z).
Axes of the slice: x: 4, y: 4, z: 8, core: 2. Of those that a mesh axis runs over, the one named last changes fastest.
Arguments:
- tokens: bfloat16 [2048, 16384], P('dp'), may hold values from -9 to 9
- order: int32 [2048], replicated, may hold values from 0 to 2047, as said below
- segments: int32 [2048], replicated, may hold values from 0 to 1, as said below
- gain: float32 [2, 16384], P('section', 'dp'), may hold values from 0.1 to 1.9
- w_query: bfloat16 [2, 16384, 8192], P('section', 'dp', 'tensor'), may hold values from -0.046875 to 0.046875
- key_value_weight: bfloat16 [2, 16384, 8, 256], P('section', 'dp', 'tensor'), may hold values from -0.046875 to 0.046875
- w_out: bfloat16 [2, 8192, 16384], P('section', 'tensor', 'dp'), may hold values from -0.0625 to 0.0625
Outputs:
- layer_out: bfloat16 [2048, 16384], P('section', 'dp')
Inputs may be any that keep to these rules, and one draw needn't show every extreme that they name: A permutation that moves whole sentences: the rows of one sentence (a run of equal segments within a block of 32 rows) come from consecutive entry rows in order. `segments`: within each block of 32 rows the sentence numbers do not fall and each of 0 to 1 appears.
All inputs are finite; a program needn't handle non-finite values.
Results may differ from a plain program's by a relative error of at most 0.022.
Values may be sent and summed in bfloat16 or wider, within the bound.
No kernel may reach another device: no remote copies, remote signals or barrier semaphores. Data moves between devices by JAX's collectives and lax.ppermute only.
A program may use at most 64 MiB of HBM per device.

v0:
```python
import math
import jax
import jax.numpy as jnp
from jax import lax
from jax.experimental.layout import Layout, with_layout_constraint
from jax.sharding import PartitionSpec as P

MODEL_WIDTH = 16384
KEYVALUE_HEADS = 8
QUERY_HEADS = 64
MICRO_TOKENS = 32
HEAD_WIDTH = 128
SPARE_COLUMNS = 128
M = 4
norm_epsilon = 1e-05


def causal_block_attend(query_rows, key_value_rows, allowed, query_group_width):
    block_count, row_count = allowed.shape[:2]
    kv_heads = key_value_rows.shape[1]
    head_size = key_value_rows.shape[2] // 2
    query_head_rows = query_rows.reshape(
        block_count, row_count, kv_heads, query_group_width, head_size
    )
    key_value_blocks = key_value_rows.reshape(block_count, row_count, kv_heads, 2 * head_size)
    key_heads = key_value_blocks[..., :head_size]
    value_heads = key_value_blocks[..., head_size:]
    scores = jnp.einsum(
        "bqkgd,bskd->bkgqs", query_head_rows, key_heads, preferred_element_type=jnp.float32
    ) / math.sqrt(head_size)
    raw_weights = jnp.where(allowed[:, None, None], jnp.exp(scores), 0.0)
    totals = jnp.sum(raw_weights, axis=-1, keepdims=True)
    probs = (raw_weights / totals).astype(jnp.bfloat16)
    attended_rows = jnp.einsum(
        "bkgqs,bskd->bqkgd", probs, value_heads, preferred_element_type=jnp.float32
    )
    return attended_rows.astype(jnp.bfloat16).reshape(
        block_count * row_count, kv_heads * query_group_width * head_size
    )


def block_mask(sentence_segment_rows):
    row_count = sentence_segment_rows.shape[1]
    position = jnp.arange(row_count)
    return (sentence_segment_rows[:, :, None] == sentence_segment_rows[:, None, :]) & (
        position[None, :] <= position[:, None]
    )[None]


def gathered_over(block, axis):
    count = lax.axis_size(axis)
    spread = jnp.broadcast_to(block[None], (count,) + block.shape)
    return lax.all_to_all(spread, axis, 0, 0, tiled=False).reshape(
        (count * block.shape[0],) + block.shape[1:]
    )


def section_layer(hidden, own_allowed, gain_row, joined_weight, out_weight):
    row_count = hidden.shape[0]
    group_count = lax.axis_size("dp")
    own_rows = row_count // group_count
    widened = hidden.astype(jnp.float32)
    normed_rows = (widened * gain_row[None, :]).astype(jnp.bfloat16)
    joined_terms = jnp.dot(normed_rows, joined_weight, preferred_element_type=jnp.float32)
    query_width = out_weight.shape[0]
    keyval_width = joined_terms.shape[1] - query_width - SPARE_COLUMNS
    square_terms = jnp.sum(widened * widened, axis=1, keepdims=True)
    square_high = lax.reduce_precision(square_terms, exponent_bits=8, mantissa_bits=7)
    square_low = square_terms - square_high
    column = lax.broadcasted_iota(jnp.int32, joined_terms.shape, 1)
    square_column = query_width + keyval_width
    payload = jnp.where(
        column == square_column,
        square_high,
        jnp.where(column == square_column + 1, square_low, joined_terms),
    ).astype(jnp.bfloat16)
    arrived = lax.all_to_all(
        payload.reshape(group_count, own_rows, payload.shape[1]), "dp", 0, 0, tiled=False
    )
    summed = jnp.sum(arrived.astype(jnp.float32), axis=0)
    own_squares = summed[:, query_width + keyval_width] + summed[:, query_width + keyval_width + 1]
    root_mean_square = jnp.sqrt(own_squares / MODEL_WIDTH + norm_epsilon)
    scaled_sums = summed[:, : query_width + keyval_width] / root_mean_square[:, None]
    query_rows = scaled_sums[:, :query_width].astype(jnp.bfloat16)
    key_value_rows = (
        scaled_sums[:, query_width:].astype(jnp.bfloat16).reshape(own_rows, -1, 2 * HEAD_WIDTH)
    )
    attended_rows = causal_block_attend(
        query_rows, key_value_rows, own_allowed, QUERY_HEADS // KEYVALUE_HEADS
    )
    head_terms = jnp.dot(
        gathered_over(attended_rows, "dp"), out_weight, preferred_element_type=jnp.float32
    )
    head_total = lax.psum(head_terms.astype(jnp.bfloat16), "tensor").astype(jnp.float32)
    return (widened + head_total).astype(jnp.bfloat16)


def on_device(tokens, order, segments, gain, w_query, key_value_weight, w_out):
    section_count = lax.axis_size("section")
    section_index = lax.axis_index("section")
    group_count = lax.axis_size("dp")
    slice_width = w_query.shape[1]
    joined = jnp.concatenate(
        [
            w_query[0],
            key_value_weight[0].reshape(slice_width, -1),
            jnp.zeros((slice_width, SPARE_COLUMNS), w_query.dtype),
        ],
        axis=1,
    )
    own = (gain[0], joined, w_out[0])
    swap = [(i, (i + 1) % section_count) for i in range(section_count)]
    other = lax.ppermute(own, "section", swap)
    entry_rows, model_width = tokens.shape
    part_rows = entry_rows // section_count
    my_rows = lax.dynamic_slice_in_dim(tokens, section_index * part_rows, part_rows)
    got = lax.all_to_all(
        my_rows.reshape(part_rows, group_count, model_width // group_count), "dp", 1, 0, tiled=True
    ).reshape(group_count * part_rows, -1)
    received = lax.ppermute(got, "section", swap)
    rows_here = group_count * entry_rows // section_count
    own_blocks = rows_here // (group_count * MICRO_TOKENS)
    own_segments = lax.dynamic_slice_in_dim(
        segments,
        section_index * rows_here + lax.axis_index("dp") * own_blocks * MICRO_TOKENS,
        own_blocks * MICRO_TOKENS,
    ).reshape(own_blocks, MICRO_TOKENS)
    other, received, own_allowed = lax.optimization_barrier(
        (other, received, block_mask(own_segments))
    )
    my_order = lax.dynamic_slice_in_dim(order, section_index * rows_here, rows_here)
    source_group = my_order // entry_rows
    within = my_order % entry_rows
    from_other = within // part_rows != section_index
    block_index = source_group * part_rows + within % part_rows
    hits = lax.broadcasted_iota(jnp.int32, (rows_here, got.shape[0]), 1) == block_index[:, None]
    picked_here = (hits & ~from_other[:, None]).astype(got.dtype)
    picked_there = (hits & from_other[:, None]).astype(got.dtype)
    hidden = (
        jnp.dot(picked_here, got, preferred_element_type=jnp.float32)
        + jnp.dot(picked_there, received, preferred_element_type=jnp.float32)
    ).astype(got.dtype)
    hidden = with_layout_constraint(hidden, Layout(major_to_minor=(0, 1)))
    for layer_index in range(section_count):
        params = jax.tree.map(
            lambda mine, theirs: jnp.where(section_index == layer_index, mine, theirs), own, other
        )
        hidden = section_layer(hidden, own_allowed, *params)
    return hidden


def solution(mesh):
    placed = (
        P("dp", None),
        P(),
        P(),
        P("section", "dp"),
        P("section", "dp", "tensor"),
        P("section", "dp", "tensor", None),
        P("section", "tensor", "dp"),
    )
    return jax.shard_map(
        on_device, mesh=mesh, in_specs=placed, out_specs=P("section", "dp"), check_vma=False
    )
```

profile of v0, /device:TPU:2, one launch (start us, length us, event | category | flops | bytes accessed | tf_op | source)
XLA Modules:
  0.0 392.8 jit_solution(6139880613853147727)
XLA Ops:
  6.5 1.7 constant_dynamic-slice_fusion
  8.3 1.6 copy.54
  9.8 7.7 %all-to-all-start = ((bf16[64,16,1024]{2,0,1:T(8,128)(2,1)}), bf16[64,16,1024]{2,0,1:T(8,128)(2,1)}, u32[]{:S(2)}, u32[]{:S(2)}) async-start(bf16[64,16,1024]{2,0,1:T(8,128)(2,1)} %bitcast.102), calls=%async_computation | async-start | bytes 4194304 | tf_op jit(solution)/shard_map/all_to_all | solution.py:117
  17.7 2.2 maximum_maximum_fusion
  19.9 0.5 collective-permute-start.2
  20.4 24.4 %all-to-all-done = bf16[64,16,1024]{2,0,1:T(8,128)(2,1)} async-done(((bf16[64,16,1024]{2,0,1:T(8,128)(2,1)}), bf16[64,16,1024]{2,0,1:T(8,128)(2,1)}, u32[]{:S(2)}, u32[]{:S(2)}) %all-to-all-start) | async-done | bytes 2097184 | tf_op jit(solution)/shard_map/all_to_all | solution.py:117
  44.8 0.5 collective-permute-start
  45.3 0.8 dynamic_slice.11
  46.3 4.0 %fusion.8 = f32[1024,1024]{1,0:T(8,128)S(1)} fusion(bf16[1024,1024]{1,0:T(8,128)(2,1)} %bitcast.2, s32[1024]{0:T(1024)S(1)} %fusion.61, pred[1024]{0:T(1024)(128)(4,1)S(1)} %get-tuple-element.15), kind=kOutput, calls=%fused_computation.20 | convolution fusion | flops 2149580800 | bytes 6296576 | tf_op jit(solution)/shard_map/dot_general | solution.py:140
  50.4 4.9 %fusion = (f32[1024]{0:T(1024)S(1)}, bf16[1024,1024]{1,0:T(8,128)(2,1)S(1)}) fusion(f32[1024,1024]{1,0:T(8,128)S(1)} %fusion.8, bf16[1024,1024]{1,0:T(8,128)(2,1)} %collective-permute-done.3, s32[1024]{0:T(1024)S(1)} %fusion.61, pred[1024]{0:T(1024)(128)(4,1)S(1)} %get-tuple-element.16), kind=kOutput, calls=%fused_computation.10 | convolution fusion | flops 2154822656 | bytes 8397824 | tf_op jit(solution)/shard_map/dot_general | solution.py:141
  55.3 3.6 select_convert_fusion.1
  58.9 44.4 %all_to_all.35 = bf16[16,64,1408]{2,1,0:T(8,128)(2,1)S(1)} all-to-all(bf16[16,64,1408]{2,1,0:T(8,128)(2,1)S(1)} %bitcast.107), channel_id=1, replica_groups=mesh['dp'=16,'section'=2,'tensor'=8] {'dp'}, dimensions={0} | all-to-all | bytes 5767168 | tf_op jit(solution)/shard_map/all_to_all | solution.py:77
  103.3 0.4 convert_reduce_fusion.1
  104.9 32.2 %all_to_all.36 = bf16[16,64,1024]{2,1,0:T(8,128)(2,1)S(1)} all-to-all(bf16[16,64,1024]{2,1,0:T(8,128)(2,1)S(1)} %broadcast_in_dim.78), channel_id=1, replica_groups=mesh['dp'=16,'section'=2,'tensor'=8] {'dp'}, dimensions={0} | all-to-all | bytes 4194304 | tf_op jit(solution)/shard_map/all_to_all | solution.py:53
  137.1 5.3 %fusion.30 = bf16[1024,1024]{1,0:T(8,128)(2,1)} fusion(bf16[1024,1024]{1,0:T(8,128)(2,1)S(1)} %bitcast.112, bf16[1024,1024]{1,0:T(8,128)(2,1)} %collective-permute-done.2, pred[]{:T(512)S(6)} %eq.58, bf16[1,1024,1024]{2,1,0:T(8,128)(2,1)} %param.13), kind=kOutput, calls=%fused_computation.40 | convolution fusion | flops 2149580800 | bytes 8388609 | tf_op jit(solution)/shard_map/dot_general | solution.py:91
  142.4 82.2 %all-reduce.3.cloned.1.call-done = bf16[1024,1024]{1,0:T(8,128)(2,1)} async-done(((bf16[1024,1024]{1,0:T(8,128)(2,1)}), bf16[1024,1024]{1,0:T(8,128)(2,1)}) %all-reduce.3.cloned.1.call-update) | async-done | bytes 2097168 | tf_op jit(solution)/shard_map/psum | solution.py:94
  224.6 2.5 fusion.3
  227.5 5.4 %select_convert_fusion = bf16[1024,1408]{1,0:T(8,128)(2,1)S(1)} fusion(bf16[1024,1408]{1,0:T(8,128)(2,1)} %collective-permute-done.1, bf16[1024]{0:T(1024)(128)(2,1)S(1)} %get-tuple-element.20, bf16[1024]{0:T(1024)(128)(2,1)S(1)} %get-tuple-element.19, pred[]{:T(512)S(6)} %eq.59, pred[1408]{0:T(1024)(128)(4,1)S(1)} %get-tuple-element.29, ...), kind=kOutput, calls=%fused_computation.7 | convolution fusion | flops 2973106176 | bytes 12596737 | tf_op jit(solution)/shard_map/dot_general | solution.py:64
  232.9 37.0 %all_to_all.37 = bf16[16,64,1408]{2,1,0:T(8,128)(2,1)S(1)} all-to-all(bf16[16,64,1408]{2,1,0:T(8,128)(2,1)S(1)} %bitcast.106), channel_id=1, replica_groups=mesh['dp'=16,'section'=2,'tensor'=8] {'dp'}, dimensions={0} | all-to-all | bytes 5767168 | tf_op jit(solution)/shard_map/all_to_all | solution.py:77
  269.8 0.4 convert_reduce_fusion
  271.5 25.5 %all_to_all.38 = bf16[16,64,1024]{2,1,0:T(8,128)(2,1)S(1)} all-to-all(bf16[16,64,1024]{2,1,0:T(8,128)(2,1)S(1)} %broadcast_in_dim.82), channel_id=1, replica_groups=mesh['dp'=16,'section'=2,'tensor'=8] {'dp'}, dimensions={0} | all-to-all | bytes 4194304 | tf_op jit(solution)/shard_map/all_to_all | solution.py:53
  297.0 5.9 %fusion.33 = bf16[1024,1024]{1,0:T(8,128)(2,1)} fusion(bf16[1024,1024]{1,0:T(8,128)(2,1)S(1)} %bitcast.111, bf16[1024,1024]{1,0:T(8,128)(2,1)} %collective-permute-done.2, pred[]{:T(512)S(6)} %eq.59, bf16[1,1024,1024]{2,1,0:T(8,128)(2,1)} %param.13), kind=kOutput, calls=%fused_computation.41 | convolution fusion | flops 2149580800 | bytes 8388609 | tf_op jit(solution)/shard_map/dot_general | solution.py:91
  302.9 78.0 %all-reduce.5.cloned.1.call-done = bf16[1024,1024]{1,0:T(8,128)(2,1)} async-done(((bf16[1024,1024]{1,0:T(8,128)(2,1)}), bf16[1024,1024]{1,0:T(8,128)(2,1)}) %all-reduce.5.cloned.1.call-update) | async-done | bytes 2097168 | tf_op jit(solution)/shard_map/psum | solution.py:94
  380.9 5.0 %fusion.5 = bf16[1024,1024]{1,0:T(8,128)(2,1)} fusion(bf16[1024,1024]{1,0:T(8,128)(2,1)} %all-reduce.5.cloned.1.call-done, bf16[1024,1024]{1,0:T(8,128)(2,1)} %all-reduce.3.cloned.1.call-done, bf16[1024,1024]{1,0:T(8,128)(2,1)S(1)} %get-tuple-element.24), kind=kLoop, calls=%fused_computation.15 | loop fusion | flops 8388608 | bytes 8388608 | tf_op jit(solution)/shard_map/convert_element_type | solution.py:95
  (55 shorter events, 3.2 us)
Async XLA Ops:
  9.8 7.8 %copy-start.1 = (bf16[1,1024,1024]{2,1,0:T(8,128)(2,1)S(1)}, bf16[1,1024,1024]{2,1,0:T(8,128)(2,1)}, u32[]{:S(2)}) copy-start(bf16[1,1024,1024]{2,1,0:T(8,128)(2,1)} %param.11) | copy-start | bytes 6291460
  9.8 7.8 %copy-start.4 = (bf16[1,1024,1,256]{3,1,2,0:T(8,128)(2,1)S(1)}, bf16[1,1024,1,256]{3,1,2,0:T(8,128)(2,1)}, u32[]{:S(2)}) copy-start(bf16[1,1024,1,256]{3,1,2,0:T(8,128)(2,1)} %param.12) | copy-start | bytes 1572868
  9.8 35.0 %all-to-all-start = ((bf16[64,16,1024]{2,0,1:T(8,128)(2,1)}), bf16[64,16,1024]{2,0,1:T(8,128)(2,1)}, u32[]{:S(2)}, u32[]{:S(2)}) async-start(bf16[64,16,1024]{2,0,1:T(8,128)(2,1)} %bitcast.102), calls=%async_computation | async-start | bytes 4194304 | tf_op jit(solution)/shard_map/all_to_all | solution.py:117
  17.6 27.2 %copy-start.6 = (f32[1,1024]{1,0:T(1,128)S(1)}, f32[1,1024]{1,0:T(1,128)}, u32[]{:S(2)}) copy-start(f32[1,1024]{1,0:T(1,128)} %param.10) | copy-start | bytes 12292
  17.6 28.6 %copy-start.5 = (s32[2048]{0:T(1024)S(1)}, s32[2048]{0:T(1024)}, u32[]{:S(2)}) copy-start(s32[2048]{0:T(1024)} %param.8) | copy-start | bytes 24580
  17.6 207.0 %all-reduce.3.cloned.1.call-start = ((), (), s32[]{:S(2)}) async-start(), calls=%async_computation.5 | async-start | bytes 4194304 | tf_op jit(solution)/shard_map/psum | solution.py:94
  19.9 30.4 %collective-permute-start.1 = (bf16[1024,1408]{1,0:T(8,128)(2,1)}, bf16[1024,1408]{1,0:T(8,128)(2,1)}, u32[]{:S(2)}, u32[]{:S(2)}) collective-permute-start(bf16[1024,1408]{1,0:T(8,128)(2,1)} %maximum_maximum_fusion), channel_id=1, source_target_pairs={{0,8},{8,0},{1,9},{9,1},{2,10},{10,2},{3,11},{11,3},{4,12},{12,4},... | collective-permute-start | bytes 8650760 | tf_op jit(solution)/shard_map/ppermute | solution.py:113
  19.9 30.4 %collective-permute-start.2 = (bf16[1024,1024]{1,0:T(8,128)(2,1)}, bf16[1024,1024]{1,0:T(8,128)(2,1)}, u32[]{:S(2)}, u32[]{:S(2)}) collective-permute-start(bf16[1024,1024]{1,0:T(8,128)(2,1)} %bitcast.6), channel_id=1, source_target_pairs={{0,8},{8,0},{1,9},{9,1},{2,10},{10,2},{3,11},{11,3},{4,12},{12,4},... | collective-permute-start | bytes 6291464 | tf_op jit(solution)/shard_map/ppermute | solution.py:113
  44.8 5.5 %collective-permute-start.3 = (bf16[1024,1024]{1,0:T(8,128)(2,1)}, bf16[1024,1024]{1,0:T(8,128)(2,1)}, u32[]{:S(2)}, u32[]{:S(2)}) collective-permute-start(bf16[1024,1024]{1,0:T(8,128)(2,1)} %bitcast.2), channel_id=1, source_target_pairs={{0,8},{8,0},{1,9},{9,1},{2,10},{10,2},{3,11},{11,3},{4,12},{12,4},... | collective-permute-start | bytes 6291464 | tf_op jit(solution)/shard_map/ppermute | solution.py:120
  44.8 5.5 %collective-permute-start = (f32[1024]{0:T(1024)S(1)}, f32[1024]{0:T(1024)S(1)}, u32[]{:S(2)}, u32[]{:S(2)}) collective-permute-start(f32[1024]{0:T(1024)S(1)} %bitcast.126), channel_id=1, source_target_pairs={{0,8},{8,0},{1,9},{9,1},{2,10},{10,2},{3,11},{11,3},{4,12},{12,4},... | collective-permute-start | bytes 12296 | tf_op jit(solution)/shard_map/ppermute | solution.py:113
  50.3 4.9 %copy-start.2 = (bf16[1,1024,1024]{2,1,0:T(8,128)(2,1)S(1)}, bf16[1,1024,1024]{2,1,0:T(8,128)(2,1)}, u32[]{:S(2)}) copy-start(bf16[1,1024,1024]{2,1,0:T(8,128)(2,1)} %param.11) | copy-start | bytes 6291460
  142.4 238.5 %all-reduce.5.cloned.1.call-start = ((), (), s32[]{:S(2)}) async-start(), calls=%async_computation.6 | async-start | bytes 4194304 | tf_op jit(solution)/shard_map/psum | solution.py:94
  224.6 2.5 copy-start
  224.6 2.9 copy-start.3
Sparse Core Ops, SparseCore 0:
  142.5 82.0 all-reduce.2
  303.1 77.8 all-reduce.4
where the time goes:
time: 393 us
  waiting for transfers between devices  185 us (47%)
  blocking collectives  139 us (35%)
  matrix products  30.1 us (8%)
  between operations  13.7 us (3%)
  other arithmetic  11.2 us (3%)
  starting transfers between devices  8.84 us (2%)
  local copies, waits for them, and re-layouts  5.23 us (1%)
    psum x2, waiting for transfers between devices, section_layer(): lax.psum(head_terms.astype(jnp.bfloat16), 'tensor').astype(jnp.float32)  160 us
    all_to_all x2, blocking collectives, section_layer(): lax.all_to_all(payload.reshape(group_count, own_rows, payload.shape[1]),...  81.4 us
    all_to_all x2, blocking collectives, gathered_over(): lax.all_to_all(spread, axis, 0, 0, tiled=False)  57.7 us
    all_to_all x1, waiting for transfers between devices, on_device(): lax.all_to_all(my_rows.reshape(part_rows, group_count, model_width // gro...  24.4 us
    dot_general x2, matrix products, section_layer(): jnp.dot(gathered_over(attended_rows, 'dp'), out_weight, preferred_element...  11.2 us
    dot_general x2, matrix products, section_layer(): jnp.dot(normed_rows, joined_weight, preferred_element_type=jnp.float32)  8.97 us
  transfers between devices with their start and end apart: 7, of which 3 were waited for; matrix products, arithmetic and copies ran while one was open for 2% of the time, Pallas kernels for 0%

commit v1 on v0

--- a/solution.py
+++ b/solution.py
@@ -114,8 +114,14 @@
     entry_rows, model_width = tokens.shape
     part_rows = entry_rows // section_count
     my_rows = lax.dynamic_slice_in_dim(tokens, section_index * part_rows, part_rows)
-    got = lax.all_to_all(
-        my_rows.reshape(part_rows, group_count, model_width // group_count), "dp", 1, 0, tiled=True
+    quarters_direct = lambda matrix, which_dim, at_axis: jnp.concatenate(
+        lax.all_to_all(
+            jnp.stack(jnp.split(matrix, lax.axis_size("dp"), axis=which_dim)), "dp", 0, 0
+        ),
+        axis=at_axis,
+    )
+    got = quarters_direct(
+        my_rows.reshape(part_rows, group_count, model_width // group_count), 1, 0
     ).reshape(group_count * part_rows, -1)
     received = lax.ppermute(got, "section", swap)
     rows_here = group_count * entry_rows // section_count

time: 393 us -> 408 us (1.038)
  local copies, waits for them, and re-layouts: 5.23 us -> 20.6 us
    unnamed x20 -> x34, local copies, waits for them, and re-layouts: 0.47 us -> 12.2 us
    split x0 -> x1, local copies, waits for them, and re-layouts: none -> 4.5 us  [on_device(): jnp.split(matrix, lax.axis_size('dp'), axis=which_dim)]
where the time goes in v1:
time: 408 us
  waiting for transfers between devices  184 us (45%)
  blocking collectives  139 us (34%)
  matrix products  30.1 us (7%)
  local copies, waits for them, and re-layouts  20.6 us (5%)
  between operations  13.8 us (3%)
  other arithmetic  11.2 us (3%)
  starting transfers between devices  9.01 us (2%)
    psum x2, waiting for transfers between devices, section_layer(): lax.psum(head_terms.astype(jnp.bfloat16), 'tensor').astype(jnp.float32)  160 us
    all_to_all x2, blocking collectives, section_layer(): lax.all_to_all(payload.reshape(group_count, own_rows, payload.shape[1]),...  81.3 us
    all_to_all x2, blocking collectives, gathered_over(): lax.all_to_all(spread, axis, 0, 0, tiled=False)  57.5 us
    all_to_all x1, waiting for transfers between devices, on_device(): lax.all_to_all(jnp.stack(jnp.split(matrix, lax.axis_size('dp'), axis=whic...  24.3 us
    unnamed x34, local copies, waits for them, and re-layouts  12.2 us
    dot_general x2, matrix products, section_layer(): jnp.dot(gathered_over(attended_rows, 'dp'), out_weight, preferred_element...  11.2 us
    dot_general x2, matrix products, section_layer(): jnp.dot(normed_rows, joined_weight, preferred_element_type=jnp.float32)  8.97 us
  transfers between devices with their start and end apart: 7, of which 3 were waited for; matrix products, arithmetic and copies ran while one was open for 2% of the time, Pallas kernels for 0%

profile of v1, /device:TPU:2, one launch (start us, length us, event | category | flops | bytes accessed | tf_op | source)
XLA Modules:
  0.0 407.7 jit_solution(14749154020659762271)
XLA Ops:
  6.5 1.7 constant_dynamic-slice_fusion
  8.3 1.2 copy.236
  9.5 4.5 %fusion.71 = (bf16[64,1,1024]{2,1,0:T(2,128)(2,1)S(1)}, bf16[64,1,1024]{2,1,0:T(2,128)(2,1)S(1)}, bf16[64,1,1024]{2,1,0:T(2,128)(2,1)S(1)}, bf16[64,1,1024]{2,1,...) fusion(bf16[64,16,1024]{2,1,0:T(8,128)(2,1)S(1)} %bitcast.131), kind=kLoop, calls=%fused_computation.127 | loop fusion | bytes 4194304 | tf_op jit(solution)/shard_map/split | solution.py:119
  14.0 0.7 bitcast_dynamic-update-slice_fusion.15
  14.7 0.7 bitcast_dynamic-update-slice_fusion.14
  16.8 0.7 bitcast_dynamic-update-slice_fusion.11
  25.2 7.6 %all-to-all-start = ((bf16[16,64,1,1024]{3,1,2,0:T(8,128)(2,1)}), bf16[16,64,1,1024]{3,1,2,0:T(8,128)(2,1)}, u32[]{:S(2)}, u32[]{:S(2)}) async-start(bf16[16,64,1,1024]{3,1,2,0:T(8,128)(2,1)} %bitcast_dynamic-update-slice_fusion), calls=%async_computation | async-start | bytes 4194304 | tf_op jit(solution)/shard_map/all_to_all | solution.py:118
  32.9 2.2 maximum_maximum_fusion
  35.7 24.3 %all-to-all-done = bf16[16,64,1,1024]{3,1,2,0:T(8,128)(2,1)} async-done(((bf16[16,64,1,1024]{3,1,2,0:T(8,128)(2,1)}), bf16[16,64,1,1024]{3,1,2,0:T(8,128)(2,1)}, u32[]{:S(2)}, u32[]{:S(2)}) %all-to-all-start) | async-done | bytes 2097184 | tf_op jit(solution)/shard_map/all_to_all | solution.py:118
  60.5 0.8 dynamic_slice.11
  61.6 4.0 fusion.8
  65.6 4.9 %fusion = (f32[1024]{0:T(1024)S(1)}, bf16[1024,1024]{1,0:T(8,128)(2,1)S(1)}) fusion(f32[1024,1024]{1,0:T(8,128)S(1)} %fusion.8, bf16[1024,1024]{1,0:T(8,128)(2,1)} %collective-permute-done.3, s32[1024]{0:T(1024)S(1)} %fusion.61, pred[1024]{0:T(1024)(128)(4,1)S(1)} %get-tuple-element.16), kind=kOutput, calls=%fused_computation.10 | convolution fusion | flops 2154822656 | bytes 8397824 | tf_op jit(solution)/shard_map/dot_general | solution.py:147
  70.5 3.6 select_convert_fusion.1
  74.1 44.4 %all_to_all.25 = bf16[16,64,1408]{2,1,0:T(8,128)(2,1)S(1)} all-to-all(bf16[16,64,1408]{2,1,0:T(8,128)(2,1)S(1)} %bitcast.134), channel_id=1, replica_groups=mesh['dp'=16,'section'=2,'tensor'=8] {'dp'}, dimensions={0} | all-to-all | bytes 5767168 | tf_op jit(solution)/shard_map/all_to_all | solution.py:77
  120.2 32.0 %all_to_all.26 = bf16[16,64,1024]{2,1,0:T(8,128)(2,1)S(1)} all-to-all(bf16[16,64,1024]{2,1,0:T(8,128)(2,1)S(1)} %broadcast_in_dim.78), channel_id=1, replica_groups=mesh['dp'=16,'section'=2,'tensor'=8] {'dp'}, dimensions={0} | all-to-all | bytes 4194304 | tf_op jit(solution)/shard_map/all_to_all | solution.py:53
  152.2 5.3 %fusion.30 = bf16[1024,1024]{1,0:T(8,128)(2,1)} fusion(bf16[1024,1024]{1,0:T(8,128)(2,1)S(1)} %bitcast.139, bf16[1024,1024]{1,0:T(8,128)(2,1)} %collective-permute-done.2, pred[]{:T(512)S(6)} %eq.58, bf16[1,1024,1024]{2,1,0:T(8,128)(2,1)} %param.13), kind=kOutput, calls=%fused_computation.39 | convolution fusion | flops 2149580800 | bytes 8388609 | tf_op jit(solution)/shard_map/dot_general | solution.py:91
  157.7 81.9 %all-reduce.3.cloned.1.call-done = bf16[1024,1024]{1,0:T(8,128)(2,1)} async-done(((bf16[1024,1024]{1,0:T(8,128)(2,1)}), bf16[1024,1024]{1,0:T(8,128)(2,1)}) %all-reduce.3.cloned.1.call-update) | async-done | bytes 2097168 | tf_op jit(solution)/shard_map/psum | solution.py:94
  239.6 2.5 fusion.3
  242.5 5.4 %select_convert_fusion = bf16[1024,1408]{1,0:T(8,128)(2,1)S(1)} fusion(bf16[1024,1408]{1,0:T(8,128)(2,1)} %collective-permute-done.1, bf16[1024]{0:T(1024)(128)(2,1)S(1)} %get-tuple-element.36, bf16[1024]{0:T(1024)(128)(2,1)S(1)} %get-tuple-element.35, pred[]{:T(512)S(6)} %eq.59, pred[1408]{0:T(1024)(128)(4,1)S(1)} %get-tuple-element.45, ...), kind=kOutput, calls=%fused_computation.7 | convolution fusion | flops 2973106176 | bytes 12596737 | tf_op jit(solution)/shard_map/dot_general | solution.py:64
  247.9 37.0 %all_to_all.27 = bf16[16,64,1408]{2,1,0:T(8,128)(2,1)S(1)} all-to-all(bf16[16,64,1408]{2,1,0:T(8,128)(2,1)S(1)} %bitcast.133), channel_id=1, replica_groups=mesh['dp'=16,'section'=2,'tensor'=8] {'dp'}, dimensions={0} | all-to-all | bytes 5767168 | tf_op jit(solution)/shard_map/all_to_all | solution.py:77
  286.5 25.5 %all_to_all.28 = bf16[16,64,1024]{2,1,0:T(8,128)(2,1)S(1)} all-to-all(bf16[16,64,1024]{2,1,0:T(8,128)(2,1)S(1)} %broadcast_in_dim.82), channel_id=1, replica_groups=mesh['dp'=16,'section'=2,'tensor'=8] {'dp'}, dimensions={0} | all-to-all | bytes 4194304 | tf_op jit(solution)/shard_map/all_to_all | solution.py:53
  312.0 5.9 %fusion.33 = bf16[1024,1024]{1,0:T(8,128)(2,1)} fusion(bf16[1024,1024]{1,0:T(8,128)(2,1)S(1)} %bitcast.138, bf16[1024,1024]{1,0:T(8,128)(2,1)} %collective-permute-done.2, pred[]{:T(512)S(6)} %eq.59, bf16[1,1024,1024]{2,1,0:T(8,128)(2,1)} %param.13), kind=kOutput, calls=%fused_computation.40 | convolution fusion | flops 2149580800 | bytes 8388609 | tf_op jit(solution)/shard_map/dot_general | solution.py:91
  318.0 77.9 %all-reduce.5.cloned.1.call-done = bf16[1024,1024]{1,0:T(8,128)(2,1)} async-done(((bf16[1024,1024]{1,0:T(8,128)(2,1)}), bf16[1024,1024]{1,0:T(8,128)(2,1)}) %all-reduce.5.cloned.1.call-update) | async-done | bytes 2097168 | tf_op jit(solution)/shard_map/psum | solution.py:94
  395.8 5.0 %fusion.5 = bf16[1024,1024]{1,0:T(8,128)(2,1)} fusion(bf16[1024,1024]{1,0:T(8,128)(2,1)} %all-reduce.5.cloned.1.call-done, bf16[1024,1024]{1,0:T(8,128)(2,1)} %all-reduce.3.cloned.1.call-done, bf16[1024,1024]{1,0:T(8,128)(2,1)S(1)} %get-tuple-element.40), kind=kLoop, calls=%fused_computation.15 | loop fusion | flops 8388608 | bytes 8388608 | tf_op jit(solution)/shard_map/convert_element_type | solution.py:95
  (70 shorter events, 14.4 us)
Async XLA Ops:
  25.2 7.7 %copy-start.3 = (bf16[1,1024,1,256]{3,1,2,0:T(8,128)(2,1)S(1)}, bf16[1,1024,1,256]{3,1,2,0:T(8,128)(2,1)}, u32[]{:S(2)}) copy-start(bf16[1,1024,1,256]{3,1,2,0:T(8,128)(2,1)} %param.12) | copy-start | bytes 1572868
  25.2 34.8 %all-to-all-start = ((bf16[16,64,1,1024]{3,1,2,0:T(8,128)(2,1)}), bf16[16,64,1,1024]{3,1,2,0:T(8,128)(2,1)}, u32[]{:S(2)}, u32[]{:S(2)}) async-start(bf16[16,64,1,1024]{3,1,2,0:T(8,128)(2,1)} %bitcast_dynamic-update-slice_fusion), calls=%async_computation | async-start | bytes 4194304 | tf_op jit(solution)/shard_map/all_to_all | solution.py:118
  32.8 206.8 %all-reduce.3.cloned.1.call-start = ((), (), s32[]{:S(2)}) async-start(), calls=%async_computation.5 | async-start | bytes 4194304 | tf_op jit(solution)/shard_map/psum | solution.py:94
  32.9 27.2 %copy-start.5 = (f32[1,1024]{1,0:T(1,128)S(1)}, f32[1,1024]{1,0:T(1,128)}, u32[]{:S(2)}) copy-start(f32[1,1024]{1,0:T(1,128)} %param.10) | copy-start | bytes 12292
  32.9 28.5 %copy-start.4 = (s32[2048]{0:T(1024)S(1)}, s32[2048]{0:T(1024)}, u32[]{:S(2)}) copy-start(s32[2048]{0:T(1024)} %param.8) | copy-start | bytes 24580
  35.1 30.4 %collective-permute-start.1 = (bf16[1024,1408]{1,0:T(8,128)(2,1)S(1)}, bf16[1024,1408]{1,0:T(8,128)(2,1)}, u32[]{:S(2)}, u32[]{:S(2)}) collective-permute-start(bf16[1024,1408]{1,0:T(8,128)(2,1)S(1)} %maximum_maximum_fusion), channel_id=1, source_target_pairs={{0,8},{8,0},{1,9},{9,1},{2,10},{10,2},{3,11},{11,3},{4,12},{12,4},... | collective-permute-start | bytes 8650760 | tf_op jit(solution)/shard_map/ppermute | solution.py:113
  35.2 30.3 %collective-permute-start.2 = (bf16[1024,1024]{1,0:T(8,128)(2,1)}, bf16[1024,1024]{1,0:T(8,128)(2,1)}, u32[]{:S(2)}, u32[]{:S(2)}) collective-permute-start(bf16[1024,1024]{1,0:T(8,128)(2,1)} %bitcast.4), channel_id=1, source_target_pairs={{0,8},{8,0},{1,9},{9,1},{2,10},{10,2},{3,11},{11,3},{4,12},{12,4},... | collective-permute-start | bytes 6291464 | tf_op jit(solution)/shard_map/ppermute | solution.py:113
  60.0 5.5 %collective-permute-start.3 = (bf16[1024,1024]{1,0:T(8,128)(2,1)}, bf16[1024,1024]{1,0:T(8,128)(2,1)}, u32[]{:S(2)}, u32[]{:S(2)}) collective-permute-start(bf16[1024,1024]{1,0:T(8,128)(2,1)} %bitcast), channel_id=1, source_target_pairs={{0,8},{8,0},{1,9},{9,1},{2,10},{10,2},{3,11},{11,3},{4,12},{12,4},... | collective-permute-start | bytes 6291464 | tf_op jit(solution)/shard_map/ppermute | solution.py:126
  60.0 5.5 %collective-permute-start = (f32[1024]{0:T(1024)S(1)}, f32[1024]{0:T(1024)S(1)}, u32[]{:S(2)}, u32[]{:S(2)}) collective-permute-start(f32[1024]{0:T(1024)S(1)} %bitcast.153), channel_id=1, source_target_pairs={{0,8},{8,0},{1,9},{9,1},{2,10},{10,2},{3,11},{11,3},{4,12},{12,4},... | collective-permute-start | bytes 12296 | tf_op jit(solution)/shard_map/ppermute | solution.py:113
  65.6 4.9 %copy-start.1 = (bf16[1,1024,1024]{2,1,0:T(8,128)(2,1)S(1)}, bf16[1,1024,1024]{2,1,0:T(8,128)(2,1)}, u32[]{:S(2)}) copy-start(bf16[1,1024,1024]{2,1,0:T(8,128)(2,1)} %param.11) | copy-start | bytes 6291460
  157.4 238.4 %all-reduce.5.cloned.1.call-start = ((), (), s32[]{:S(2)}) async-start(), calls=%async_computation.6 | async-start | bytes 4194304 | tf_op jit(solution)/shard_map/psum | solution.py:94
  239.6 2.5 copy-start
  239.6 2.9 copy-start.2
Sparse Core Ops, SparseCore 0:
  157.6 81.9 all-reduce.2
  318.1 77.7 all-reduce.4
